TPU v7x, 32 devices: a whole 2x2x4 slice. The times are simulated.
32 devices in a mesh: dp: 8 (over z, y), seq: 4 (over x, core).
Axes of the slice: x: 2, y: 2, z: 4, core: 2. Of those that a mesh axis runs over, the one named last changes fastest.
Arguments:
- frames: bfloat16 [8, 512, 1536], P('dp', 'seq'), may hold values from -6 to 6
- lengths: int32 [8, 4], P('dp'), may hold values from 1 to 256, 512 in all within a row
- ln1_gain: float32 [1536], replicated, may hold values from 0.5 to 12
- ln2_gain: float32 [1536], replicated, may hold values from 0.5 to 1.5
- w_qkv: bfloat16 [1536, 3, 1536], P('dp', None, 'seq'), may hold values from -0.15625 to 0.15625
- w_out: bfloat16 [1536, 1536], P('seq', 'dp'), may hold values from -0.15625 to 0.15625
- w_glu: bfloat16 [1536, 2, 1536], P('dp', None, 'seq'), may hold values from -0.15625 to 0.15625
- dw_kernel: bfloat16 [31, 1536], P(None, 'seq'), may hold values from -1 to 1
- w_proj: bfloat16 [1536, 1536], P('seq', 'dp'), may hold values from -0.15625 to 0.15625
Outputs:
- block_out: bfloat16 [8, 512, 1536], P('dp', 'seq')
Inputs may be any that keep to these rules, and one draw needn't show every extreme that they name: `lengths`: each row sums to 512, and its largest entry is 256.
All inputs are finite; a program needn't handle non-finite values.
Results may differ from a plain program's by a relative error of at most 0.013.
The roundings to bfloat16 on the way count: a program that leaves them out, or rounds other values in their place, can miss the bound.
Values may be sent and summed in bfloat16 or wider, within the bound.
No kernel may reach another device: no remote copies, remote signals or barrier semaphores. Data moves between devices by JAX's collectives and lax.ppermute only.
A program may use at most 64 MiB of HBM per device.

v0:
```python
import jax
import jax.numpy as jnp
from jax import lax
from jax.sharding import PartitionSpec as P

HD = 96


def layer_norm(values, gain_vec):
    mean_value = jnp.mean(values, axis=-1, keepdims=True)
    centered = values - mean_value
    variance = jnp.mean(centered * centered, axis=-1, keepdims=True)
    return (centered * lax.rsqrt(variance + 1e-05) * gain_vec).astype(jnp.bfloat16)


def segment_of(record_ends, positions):
    return jnp.sum((positions[:, None] >= record_ends[None, :]).astype(jnp.int32), axis=1)


def seq_gather(block):
    count = lax.axis_size("seq")
    me = lax.axis_index("seq")
    parts = [block]
    for shift in range(1, count):
        parts.append(lax.ppermute(block, "seq", [(i, (i - shift) % count) for i in range(count)]))
    ring = jnp.concatenate(parts + parts, axis=0)
    rows = block.shape[0]
    return lax.dynamic_slice_in_dim(ring, (count - me) % count * rows, count * rows, axis=0)


def seq_scatter_sum(full):
    count = lax.axis_size("seq")
    me = lax.axis_index("seq")
    rows = full.shape[0] // count
    total = lax.dynamic_slice_in_dim(full, me * rows, rows, axis=0).astype(jnp.float32)
    for shift in range(1, count):
        piece = lax.dynamic_slice_in_dim(full, (me + shift) % count * rows, rows, axis=0)
        got = lax.ppermute(piece, "seq", [(i, (i + shift) % count) for i in range(count)])
        total = total + got.astype(jnp.float32)
    return total


def attend(projected, seg_all, head_size):
    group_rows = projected.shape[0]
    block_rows = 512
    heads_here = projected.shape[2] // head_size
    split = projected.reshape(group_rows, 3, heads_here, head_size)
    queries = split[:, 0]
    keys = split[:, 1]
    values = split[:, 2]
    blocks = group_rows // block_rows
    scale = 1.0 / head_size**0.5

    def one_block(block_data):
        query_block, seg_block = block_data
        scores = (
            jnp.einsum("qhe,khe->hqk", query_block, keys, preferred_element_type=jnp.float32)
            * scale
        )
        allowed = seg_block[:, None] == seg_all[None, :]
        scores = jnp.where(allowed[None], scores, -1e30)
        top_score = jnp.max(scores, axis=-1, keepdims=True)
        weights = jnp.exp(scores - top_score)
        probs = (weights / jnp.sum(weights, axis=-1, keepdims=True)).astype(jnp.bfloat16)
        mixed = jnp.einsum("hqk,khe->qhe", probs, values, preferred_element_type=jnp.float32)
        return mixed.astype(jnp.bfloat16).reshape(block_rows, heads_here * head_size)

    result = lax.map(
        one_block,
        (
            queries.reshape(blocks, block_rows, heads_here, head_size),
            seg_all.reshape(blocks, block_rows),
        ),
    )
    return result.reshape(group_rows, heads_here * head_size)


def depthwise(padded, kernel, seg_here, seg_near, count):
    total_acc = jnp.zeros((count, padded.shape[1]), jnp.float32)
    for tap_index in range(kernel.shape[0]):
        window = padded[tap_index : tap_index + count].astype(jnp.float32)
        same = (seg_near[tap_index : tap_index + count] == seg_here)[:, None]
        total_acc = total_acc + jnp.where(same, window * kernel[tap_index].astype(jnp.float32), 0.0)
    return jax.nn.silu(total_acc).astype(jnp.bfloat16)


def on_device(frames, lengths, ln1_gain, ln2_gain, w_qkv, w_out, w_glu, dw_kernel, w_proj):
    frame_rows = frames.shape[1]
    model_width = frames.shape[2]
    seq_count = lax.axis_size("seq")
    group_rows = frame_rows * seq_count
    group_width = model_width // seq_count
    kernel_reach = dw_kernel.shape[0] // 2
    qkv_matrix = lax.all_gather(
        w_qkv.reshape(w_qkv.shape[0], 3 * group_width), "dp", axis=0, tiled=True
    )
    out_local = lax.all_gather(w_out, "dp", axis=1, tiled=True)
    glu_matrix = lax.all_gather(
        w_glu.reshape(w_glu.shape[0], 2 * group_width), "dp", axis=0, tiled=True
    )
    proj_local = lax.all_gather(w_proj, "dp", axis=1, tiled=True)
    inputs = frames[0].astype(jnp.float32)
    record_ends = jnp.cumsum(lengths[0])
    seg_all = segment_of(record_ends, jnp.arange(group_rows, dtype=jnp.int32))
    normed1 = layer_norm(inputs, ln1_gain)
    projected = (
        jnp.dot(seq_gather(normed1), qkv_matrix, preferred_element_type=jnp.float32)
        .astype(jnp.bfloat16)
        .reshape(group_rows, 3, group_width)
    )
    attended = attend(projected, seg_all, HD)
    attn_sum = seq_scatter_sum(
        jnp.dot(attended, out_local, preferred_element_type=jnp.float32).astype(jnp.bfloat16)
    )
    middle = (inputs + attn_sum).astype(jnp.bfloat16)
    normed2 = layer_norm(middle.astype(jnp.float32), ln2_gain)
    shard_piece = seq_gather(normed2)
    paired = jnp.dot(shard_piece, glu_matrix, preferred_element_type=jnp.float32).reshape(
        shard_piece.shape[0], 2, group_width
    )
    gated = (paired[:, 0] * jax.nn.sigmoid(paired[:, 1])).astype(jnp.bfloat16)
    padded = jnp.pad(gated, ((kernel_reach, kernel_reach), (0, 0)))
    near_positions = jnp.arange(-kernel_reach, group_rows + kernel_reach, dtype=jnp.int32)
    activated = depthwise(
        padded, dw_kernel, seg_all, segment_of(record_ends, near_positions), group_rows
    )
    conv_out = seq_scatter_sum(
        jnp.dot(activated, proj_local, preferred_element_type=jnp.float32).astype(jnp.bfloat16)
    )
    results = [(middle.astype(jnp.float32) + conv_out).astype(jnp.bfloat16)]
    return jnp.stack(results, axis=0)


def solution(mesh):
    in_specs = (
        P("dp", "seq", None),
        P("dp", None),
        P(),
        P(),
        P("dp", None, "seq"),
        P("seq", "dp"),
        P("dp", None, "seq"),
        P(None, "seq"),
        P("seq", "dp"),
    )
    out_specs = P("dp", "seq", None)
    return jax.shard_map(
        on_device, mesh=mesh, in_specs=in_specs, out_specs=out_specs, check_vma=False
    )
```

profile of v0, /device:TPU:1, one launch (start us, length us, event | category | flops | bytes accessed | tf_op | source)
XLA Modules:
  0.0 247.0 jit_solution(16871168828461402253)
XLA Ops:
  6.5 1.9 copy.27
  14.4 2.7 %collective-permute-start.1 = (bf16[128,1536]{1,0:T(8,128)(2,1)S(1)}, bf16[128,1536]{1,0:T(8,128)(2,1)S(1)}, u32[]{:S(2)}, u32[]{:S(2)}) collective-permute-start(bf16[128,1536]{1,0:T(8,128)(2,1)S(1)} %get-tuple-element.62), channel_id=1, source_target_pairs={{0,2},{1,3},{2,0},{3,1},{4,6},{5,7},{6,4},{7,5},{8,10},{9,11},{10,... | collective-permute-start | bytes 1179656 | tf_op jit(solution)/shard_map/ppermute | solution.py:25
  19.0 8.0 %collective-permute-done = bf16[128,1536]{1,0:T(8,128)(2,1)S(1)} collective-permute-done((bf16[128,1536]{1,0:T(8,128)(2,1)S(1)}, bf16[128,1536]{1,0:T(8,128)(2,1)S(1)}, u32[]{:S(2)}, u32[]{:S(2)}) %collective-permute-start) | collective-permute-done | bytes 393248 | tf_op jit(solution)/shard_map/ppermute | solution.py:25
  28.6 5.9 %collective-permute-done.2 = bf16[128,1536]{1,0:T(8,128)(2,1)S(1)} collective-permute-done((bf16[128,1536]{1,0:T(8,128)(2,1)S(1)}, bf16[128,1536]{1,0:T(8,128)(2,1)S(1)}, u32[]{:S(2)}, u32[]{:S(2)}) %collective-permute-start.2) | collective-permute-done | bytes 393248 | tf_op jit(solution)/shard_map/ppermute | solution.py:25
  38.4 37.5 %all-gather.5.cloned.1.call-done = bf16[1536,1152]{1,0:T(8,128)(2,1)} async-done(((bf16[192,1152]{1,0:T(8,128)(2,1)}), bf16[1536,1152]{1,0:T(8,128)(2,1)}) %all-gather.5.cloned.1.call-update) | async-done | bytes 3538960 | tf_op jit(solution)/shard_map/all_gather | solution.py:94
  75.9 4.7 %convolution_convert_fusion = bf16[512,1152]{1,0:T(8,128)(2,1)S(1)} fusion(bf16[1536,1152]{1,0:T(8,128)(2,1)} %all-gather.5.cloned.1.call-done, bf16[1024,1536]{1,0:T(8,128)(2,1)} %constant_dynamic-update-slice_fusion, s32[]{:T(128)S(6)} %select_n.147), kind=kOutput, calls=%fused_computation.5 | convolution fusion | flops 1812529152 | bytes 6291460 | tf_op jit(solution)/shard_map/dot_general | solution.py:107
  81.2 3.6 %fusion.45 = (f32[4,512]{1,0:T(4,128)S(1)}, f32[4,512,512]{1,2,0:T(8,128)}) fusion(pred[512,512]{0,1:T(8,128)(4,1)S(1)} %broadcast_compare_fusion, bf16[512,3,4,96]{0,3,2,1:T(8,128)(2,1)S(1)} %bitcast.65), kind=kOutput, calls=%fused_computation.155 | convolution fusion | flops 205521408 | bytes 5251072 | tf_op jit(solution)/shard_map/while/body/eval_jaxpr/sub | solution.py:63
  84.8 2.8 %fusion.9 = bf16[4,96,512]{2,1,0:T(8,128)(2,1)S(1)} fusion(f32[4,512,512]{1,2,0:T(8,128)} %get-tuple-element.103, f32[4,512]{1,0:T(4,128)S(1)} %get-tuple-element.102, bf16[512,3,4,96]{0,3,2,1:T(8,128)(2,1)S(1)} %bitcast.66), kind=kOutput, calls=%fused_computation.15 | convolution fusion | flops 203620352 | bytes 4988928 | tf_op jit(solution)/shard_map/while/body/eval_jaxpr/hqk,khe->qhe/dot_general | solution.py:65
  87.6 29.8 %all-gather.7.cloned.1.call-done = bf16[384,1536]{0,1:T(8,128)(2,1)} async-done(((bf16[384,192]{0,1:T(8,128)(2,1)}), bf16[384,1536]{0,1:T(8,128)(2,1)}) %all-gather.7.cloned.1.call-update) | async-done | bytes 1179664 | tf_op jit(solution)/shard_map/all_gather | solution.py:97
  117.4 2.3 convolution_convert_fusion.2
  119.8 3.1 %collective-permute-start.3 = (bf16[128,1536]{1,0:T(8,128)(2,1)S(1)}, bf16[128,1536]{1,0:T(8,128)(2,1)S(1)}, u32[]{:S(2)}, u32[]{:S(2)}) collective-permute-start(bf16[128,1536]{1,0:T(8,128)(2,1)S(1)} %get-tuple-element.68), channel_id=1, source_target_pairs={{0,1},{1,2},{2,3},{3,0},{4,5},{5,6},{6,7},{7,4},{8,9},{9,10},{10,1... | collective-permute-start | bytes 1179656 | tf_op jit(solution)/shard_map/ppermute | solution.py:38
  124.7 6.4 %collective-permute-done.3 = bf16[128,1536]{1,0:T(8,128)(2,1)S(1)} collective-permute-done((bf16[128,1536]{1,0:T(8,128)(2,1)S(1)}, bf16[128,1536]{1,0:T(8,128)(2,1)S(1)}, u32[]{:S(2)}, u32[]{:S(2)}) %collective-permute-start.3) | collective-permute-done | bytes 393248 | tf_op jit(solution)/shard_map/ppermute | solution.py:38
  131.2 9.5 %collective-permute-done.4 = bf16[128,1536]{1,0:T(8,128)(2,1)} collective-permute-done((bf16[128,1536]{1,0:T(8,128)(2,1)S(1)}, bf16[128,1536]{1,0:T(8,128)(2,1)}, u32[]{:S(2)}, u32[]{:S(2)}) %collective-permute-start.4) | collective-permute-done | bytes 393248 | tf_op jit(solution)/shard_map/ppermute | solution.py:38
  145.5 2.2 collective-permute-start.8
  147.8 8.0 %collective-permute-done.6 = bf16[128,1536]{1,0:T(8,128)(2,1)S(1)} collective-permute-done((bf16[128,1536]{1,0:T(8,128)(2,1)S(1)}, bf16[128,1536]{1,0:T(8,128)(2,1)S(1)}, u32[]{:S(2)}, u32[]{:S(2)}) %collective-permute-start.6) | collective-permute-done | bytes 393248 | tf_op jit(solution)/shard_map/ppermute | solution.py:25
  157.3 5.1 %collective-permute-done.8 = bf16[128,1536]{1,0:T(8,128)(2,1)S(1)} collective-permute-done((bf16[128,1536]{1,0:T(8,128)(2,1)S(1)}, bf16[128,1536]{1,0:T(8,128)(2,1)S(1)}, u32[]{:S(2)}, u32[]{:S(2)}) %collective-permute-start.8) | collective-permute-done | bytes 393248 | tf_op jit(solution)/shard_map/ppermute | solution.py:25
  166.3 4.2 %all-gather.9.cloned.1.call-done = bf16[1536,768]{1,0:T(8,128)(2,1)} async-done(((bf16[192,768]{1,0:T(8,128)(2,1)}), bf16[1536,768]{1,0:T(8,128)(2,1)}) %all-gather.9.cloned.1.call-update) | async-done | bytes 2359312 | tf_op jit(solution)/shard_map/all_gather | solution.py:98
  170.5 4.7 %fusion.6 = f32[512,768]{1,0:T(8,128)} fusion(bf16[1536,768]{1,0:T(8,128)(2,1)} %all-gather.9.cloned.1.call-done, bf16[1024,1536]{1,0:T(8,128)(2,1)} %constant_dynamic-update-slice_fusion.8, s32[]{:T(128)S(6)} %select_n.147), kind=kOutput, calls=%fused_computation.12 | convolution fusion | flops 1207959552 | bytes 5505028 | tf_op jit(solution)/shard_map/dot_general | solution.py:118
  175.1 2.1 reshape.147
  178.9 33.2 %all-gather.11.cloned.1.call-done = bf16[384,1536]{0,1:T(8,128)(2,1)} async-done(((bf16[384,192]{0,1:T(8,128)(2,1)}), bf16[384,1536]{0,1:T(8,128)(2,1)}) %all-gather.11.cloned.1.call-update) | async-done | bytes 1179664 | tf_op jit(solution)/shard_map/all_gather | solution.py:101
  212.2 7.8 %convolution_convert_fusion.1 = bf16[512,1536]{1,0:T(8,128)(2,1)S(1)} fusion(bf16[384,1536]{0,1:T(8,128)(2,1)} %all-gather.11.cloned.1.call-done, bf16[512,384]{1,0:T(8,128)(2,1)S(1)} %fusion.32, f32[384]{0:T(512)S(1)} %get-tuple-element.55, f32[384]{0:T(512)S(1)} %get-tuple-element.56, f32[384]{0:T(512)S(1)} %get-tuple-element.18, ...), kind=kOutput, calls=%fused_computation.6 | convolution fusion | flops 629932032 | bytes 3209216 | tf_op jit(solution)/shard_map/dot_general | solution.py:128
  221.4 2.2 collective-permute-start.11
  223.8 5.1 %collective-permute-done.10 = bf16[128,1536]{1,0:T(8,128)(2,1)S(1)} collective-permute-done((bf16[128,1536]{1,0:T(8,128)(2,1)S(1)}, bf16[128,1536]{1,0:T(8,128)(2,1)S(1)}, u32[]{:S(2)}, u32[]{:S(2)}) %collective-permute-start.10) | collective-permute-done | bytes 393248 | tf_op jit(solution)/shard_map/ppermute | solution.py:38
  228.9 10.6 %collective-permute-done.11 = bf16[128,1536]{1,0:T(8,128)(2,1)S(1)} collective-permute-done((bf16[128,1536]{1,0:T(8,128)(2,1)S(1)}, bf16[128,1536]{1,0:T(8,128)(2,1)S(1)}, u32[]{:S(2)}, u32[]{:S(2)}) %collective-permute-start.11) | collective-permute-done | bytes 393248 | tf_op jit(solution)/shard_map/ppermute | solution.py:38
  (108 shorter events, 30.2 us)
Async XLA Ops:
  6.5 69.3 %all-gather.5.cloned.1.call-start = ((), (), s32[]{:S(2)}) async-start(), calls=%async_computation | async-start | bytes 3981312 | tf_op jit(solution)/shard_map/all_gather | solution.py:94
  8.4 108.9 %all-gather.7.cloned.1.call-start = ((), (), s32[]{:S(2)}) async-start(), calls=%async_computation.1 | async-start | bytes 1327104 | tf_op jit(solution)/shard_map/all_gather | solution.py:97
  9.2 161.3 %all-gather.9.cloned.1.call-start = ((), (), s32[]{:S(2)}) async-start(), calls=%async_computation.2 | async-start | bytes 2654208 | tf_op jit(solution)/shard_map/all_gather | solution.py:98
  11.0 201.1 %all-gather.11.cloned.1.call-start = ((), (), s32[]{:S(2)}) async-start(), calls=%async_computation.3 | async-start | bytes 1327104 | tf_op jit(solution)/shard_map/all_gather | solution.py:101
  14.4 12.7 %collective-permute-start = (bf16[128,1536]{1,0:T(8,128)(2,1)S(1)}, bf16[128,1536]{1,0:T(8,128)(2,1)S(1)}, u32[]{:S(2)}, u32[]{:S(2)}) collective-permute-start(bf16[128,1536]{1,0:T(8,128)(2,1)S(1)} %get-tuple-element.62), channel_id=1, source_target_pairs={{0,3},{1,0},{2,1},{3,2},{4,7},{5,4},{6,5},{7,6},{8,11},{9,8},{10,9... | collective-permute-start | bytes 1179656 | tf_op jit(solution)/shard_map/ppermute | solution.py:25
  14.4 13.4 %collective-permute-start.1 = (bf16[128,1536]{1,0:T(8,128)(2,1)S(1)}, bf16[128,1536]{1,0:T(8,128)(2,1)S(1)}, u32[]{:S(2)}, u32[]{:S(2)}) collective-permute-start(bf16[128,1536]{1,0:T(8,128)(2,1)S(1)} %get-tuple-element.62), channel_id=1, source_target_pairs={{0,2},{1,3},{2,0},{3,1},{4,6},{5,7},{6,4},{7,5},{8,10},{9,11},{10,... | collective-permute-start | bytes 1179656 | tf_op jit(solution)/shard_map/ppermute | solution.py:25
  17.1 17.4 %collective-permute-start.2 = (bf16[128,1536]{1,0:T(8,128)(2,1)S(1)}, bf16[128,1536]{1,0:T(8,128)(2,1)S(1)}, u32[]{:S(2)}, u32[]{:S(2)}) collective-permute-start(bf16[128,1536]{1,0:T(8,128)(2,1)S(1)} %get-tuple-element.62), channel_id=1, source_target_pairs={{0,1},{1,2},{2,3},{3,0},{4,5},{5,6},{6,7},{7,4},{8,9},{9,10},{10,1... | collective-permute-start | bytes 1179656 | tf_op jit(solution)/shard_map/ppermute | solution.py:25
  119.8 11.4 %collective-permute-start.3 = (bf16[128,1536]{1,0:T(8,128)(2,1)S(1)}, bf16[128,1536]{1,0:T(8,128)(2,1)S(1)}, u32[]{:S(2)}, u32[]{:S(2)}) collective-permute-start(bf16[128,1536]{1,0:T(8,128)(2,1)S(1)} %get-tuple-element.68), channel_id=1, source_target_pairs={{0,1},{1,2},{2,3},{3,0},{4,5},{5,6},{6,7},{7,4},{8,9},{9,10},{10,1... | collective-permute-start | bytes 1179656 | tf_op jit(solution)/shard_map/ppermute | solution.py:38
  122.8 17.9 %collective-permute-start.4 = (bf16[128,1536]{1,0:T(8,128)(2,1)S(1)}, bf16[128,1536]{1,0:T(8,128)(2,1)}, u32[]{:S(2)}, u32[]{:S(2)}) collective-permute-start(bf16[128,1536]{1,0:T(8,128)(2,1)S(1)} %get-tuple-element.70), channel_id=1, source_target_pairs={{0,2},{1,3},{2,0},{3,1},{4,6},{5,7},{6,4},{7,5},{8,10},{9,11},{10,... | collective-permute-start | bytes 1179656 | tf_op jit(solution)/shard_map/ppermute | solution.py:38
  123.1 18.2 %collective-permute-start.5 = (bf16[128,1536]{1,0:T(8,128)(2,1)S(1)}, bf16[128,1536]{1,0:T(8,128)(2,1)}, u32[]{:S(2)}, u32[]{:S(2)}) collective-permute-start(bf16[128,1536]{1,0:T(8,128)(2,1)S(1)} %get-tuple-element.69), channel_id=1, source_target_pairs={{0,3},{1,0},{2,1},{3,2},{4,7},{5,4},{6,5},{7,6},{8,11},{9,8},{10,9... | collective-permute-start | bytes 1179656 | tf_op jit(solution)/shard_map/ppermute | solution.py:38
  144.0 11.7 %collective-permute-start.6 = (bf16[128,1536]{1,0:T(8,128)(2,1)S(1)}, bf16[128,1536]{1,0:T(8,128)(2,1)S(1)}, u32[]{:S(2)}, u32[]{:S(2)}) collective-permute-start(bf16[128,1536]{1,0:T(8,128)(2,1)S(1)} %get-tuple-element.58), channel_id=1, source_target_pairs={{0,3},{1,0},{2,1},{3,2},{4,7},{5,4},{6,5},{7,6},{8,11},{9,8},{10,9... | collective-permute-start | bytes 1179656 | tf_op jit(solution)/shard_map/ppermute | solution.py:25
  144.1 12.4 %collective-permute-start.7 = (bf16[128,1536]{1,0:T(8,128)(2,1)S(1)}, bf16[128,1536]{1,0:T(8,128)(2,1)S(1)}, u32[]{:S(2)}, u32[]{:S(2)}) collective-permute-start(bf16[128,1536]{1,0:T(8,128)(2,1)S(1)} %get-tuple-element.58), channel_id=1, source_target_pairs={{0,2},{1,3},{2,0},{3,1},{4,6},{5,7},{6,4},{7,5},{8,10},{9,11},{10,... | collective-permute-start | bytes 1179656 | tf_op jit(solution)/shard_map/ppermute | solution.py:25
  145.5 16.9 %collective-permute-start.8 = (bf16[128,1536]{1,0:T(8,128)(2,1)S(1)}, bf16[128,1536]{1,0:T(8,128)(2,1)S(1)}, u32[]{:S(2)}, u32[]{:S(2)}) collective-permute-start(bf16[128,1536]{1,0:T(8,128)(2,1)S(1)} %get-tuple-element.58), channel_id=1, source_target_pairs={{0,1},{1,2},{2,3},{3,0},{4,5},{5,6},{6,7},{7,4},{8,9},{9,10},{10,1... | collective-permute-start | bytes 1179656 | tf_op jit(solution)/shard_map/ppermute | solution.py:25
  177.3 34.8 %copy-start.5 = (pred[512]{0:T(512)(128)(4,1)S(1)}, pred[512]{0:T(512)(128)(4,1)}, u32[]{:S(2)}) copy-start(pred[512]{0:T(512)(128)(4,1)} %get-tuple-element.71) | copy-start | bytes 1540
  177.3 34.8 %copy-start.6 = (pred[512]{0:T(512)(128)(4,1)S(1)}, pred[512]{0:T(512)(128)(4,1)}, u32[]{:S(2)}) copy-start(pred[512]{0:T(512)(128)(4,1)} %get-tuple-element.72) | copy-start | bytes 1540
  177.3 34.8 %copy-start.7 = (pred[512]{0:T(512)(128)(4,1)S(1)}, pred[512]{0:T(512)(128)(4,1)}, u32[]{:S(2)}) copy-start(pred[512]{0:T(512)(128)(4,1)} %get-tuple-element.73) | copy-start | bytes 1540
  177.3 34.8 %copy-start.8 = (pred[512]{0:T(512)(128)(4,1)S(1)}, pred[512]{0:T(512)(128)(4,1)}, u32[]{:S(2)}) copy-start(pred[512]{0:T(512)(128)(4,1)} %get-tuple-element.74) | copy-start | bytes 1540
  177.3 34.8 %copy-start.9 = (pred[512]{0:T(512)(128)(4,1)S(1)}, pred[512]{0:T(512)(128)(4,1)}, u32[]{:S(2)}) copy-start(pred[512]{0:T(512)(128)(4,1)} %get-tuple-element.75) | copy-start | bytes 1540
  177.3 34.8 %copy-start.10 = (pred[512]{0:T(512)(128)(4,1)S(1)}, pred[512]{0:T(512)(128)(4,1)}, u32[]{:S(2)}) copy-start(pred[512]{0:T(512)(128)(4,1)} %get-tuple-element.76) | copy-start | bytes 1540
  177.3 34.8 %copy-start.11 = (pred[512]{0:T(512)(128)(4,1)S(1)}, pred[512]{0:T(512)(128)(4,1)}, u32[]{:S(2)}) copy-start(pred[512]{0:T(512)(128)(4,1)} %get-tuple-element.77) | copy-start | bytes 1540
  177.3 34.8 %copy-start.12 = (pred[512]{0:T(512)(128)(4,1)S(1)}, pred[512]{0:T(512)(128)(4,1)}, u32[]{:S(2)}) copy-start(pred[512]{0:T(512)(128)(4,1)} %get-tuple-element.78) | copy-start | bytes 1540
  220.2 8.7 %collective-permute-start.10 = (bf16[128,1536]{1,0:T(8,128)(2,1)S(1)}, bf16[128,1536]{1,0:T(8,128)(2,1)S(1)}, u32[]{:S(2)}, u32[]{:S(2)}) collective-permute-start(bf16[128,1536]{1,0:T(8,128)(2,1)S(1)} %get-tuple-element.65), channel_id=1, source_target_pairs={{0,2},{1,3},{2,0},{3,1},{4,6},{5,7},{6,4},{7,5},{8,10},{9,11},{10,... | collective-permute-start | bytes 1179656 | tf_op jit(solution)/shard_map/ppermute | solution.py:38
  221.4 18.1 %collective-permute-start.11 = (bf16[128,1536]{1,0:T(8,128)(2,1)S(1)}, bf16[128,1536]{1,0:T(8,128)(2,1)S(1)}, u32[]{:S(2)}, u32[]{:S(2)}) collective-permute-start(bf16[128,1536]{1,0:T(8,128)(2,1)S(1)} %get-tuple-element.64), channel_id=1, source_target_pairs={{0,3},{1,0},{2,1},{3,2},{4,7},{5,4},{6,5},{7,6},{8,11},{9,8},{10,9... | collective-permute-start | bytes 1179656 | tf_op jit(solution)/shard_map/ppermute | solution.py:38
  223.6 15.9 %collective-permute-start.9 = (bf16[128,1536]{1,0:T(8,128)(2,1)S(1)}, bf16[128,1536]{1,0:T(8,128)(2,1)S(1)}, u32[]{:S(2)}, u32[]{:S(2)}) collective-permute-start(bf16[128,1536]{1,0:T(8,128)(2,1)S(1)} %get-tuple-element.63), channel_id=1, source_target_pairs={{0,1},{1,2},{2,3},{3,0},{4,5},{5,6},{6,7},{7,4},{8,9},{9,10},{10,1... | collective-permute-start | bytes 1179656 | tf_op jit(solution)/shard_map/ppermute | solution.py:38
  (16 other events, 438.8 us)
Sparse Core Ops, SparseCore 0:
  9.5 66.2 all-gather.4
  78.1 39.2 all-gather.6
  119.5 50.8 all-gather.8
  172.5 39.5 all-gather.10
where the time goes:
time: 247 us
  waiting for transfers between devices  165 us (67%)
  matrix products  25.8 us (10%)
  local copies, waits for them, and re-layouts  18.8 us (8%)
  starting transfers between devices  14.8 us (6%)
  between operations  13.6 us (6%)
  other arithmetic  9.38 us (4%)
    all_gather x1, waiting for transfers between devices, on_device(): lax.all_gather(w_qkv.reshape(w_qkv.shape[0], 3 * group_width), 'dp', axis...  37.5 us
    all_gather x1, waiting for transfers between devices, on_device(): proj_local = lax.all_gather(w_proj, 'dp', axis=1, tiled=True)  33.2 us
    ppermute x6, waiting for transfers between devices, seq_scatter_sum(): lax.ppermute(piece, 'seq', [(i, (i + shift) % count) for i in range(count)])  32.3 us
    all_gather x1, waiting for transfers between devices, on_device(): out_local = lax.all_gather(w_out, 'dp', axis=1, tiled=True)  29.8 us
    ppermute x6, waiting for transfers between devices, seq_gather(): lax.ppermute(block, 'seq', [(i, (i - shift) % count) for i in range(count)])  26.9 us
    unnamed x61, local copies, waits for them, and re-layouts  11.2 us
    dot_general x1, matrix products, on_device(): jnp.dot(activated, proj_local, preferred_element_type=jnp.float32)  7.81 us
    ppermute x6, starting transfers between devices, seq_gather(): lax.ppermute(block, 'seq', [(i, (i - shift) % count) for i in range(count)])  7.57 us
  transfers between devices with their start and end apart: 16, of which 13 were waited for; matrix products, arithmetic and copies ran while one was open for 17% of the time, Pallas kernels for 0%

commit v1 on v0

--- a/solution.py
+++ b/solution.py
@@ -4,6 +4,19 @@
 from jax.sharding import PartitionSpec as P
 
 HD = 96
+
+
+def gather_around(shard, axis, dim):
+    ways = lax.axis_size(axis)
+    up = [(d, (d + 1) % ways) for d in range(ways)]
+    down = [(d, (d - 1) % ways) for d in range(ways)]
+    earlier, later = ([shard], [shard])
+    for _ in range(ways // 2):
+        earlier.append(lax.ppermute(earlier[-1], axis, up))
+    for _ in range((ways - 1) // 2):
+        later.append(lax.ppermute(later[-1], axis, down))
+    line = jnp.concatenate([*earlier[::-1], *later[1:]], axis=dim)
+    return jnp.roll(line, (lax.axis_index(axis) - ways // 2) * shard.shape[dim], axis=dim)
 
 
 def layer_norm(values, gain_vec):
@@ -91,9 +104,7 @@
     group_rows = frame_rows * seq_count
     group_width = model_width // seq_count
     kernel_reach = dw_kernel.shape[0] // 2
-    qkv_matrix = lax.all_gather(
-        w_qkv.reshape(w_qkv.shape[0], 3 * group_width), "dp", axis=0, tiled=True
-    )
+    qkv_matrix = gather_around(w_qkv.reshape(w_qkv.shape[0], 3 * group_width), "dp", 0)
     out_local = lax.all_gather(w_out, "dp", axis=1, tiled=True)
     glu_matrix = lax.all_gather(
         w_glu.reshape(w_glu.shape[0], 2 * group_width), "dp", axis=0, tiled=True

time: 247 us -> 213 us (0.86)
  waiting for transfers between devices: 165 us -> 116 us
  starting transfers between devices: 14.8 us -> 30.1 us
  matrix products: 25.8 us -> 22.5 us
  other arithmetic: 9.38 us -> 12.2 us
    ppermute x0 -> x7, waiting for transfers between devices: none -> 60.5 us  [the longest x4 56 us: gather_around(): earlier.append(lax.ppermute(earlier[-1], axis, up))]
    all_gather x1 -> x0, waiting for transfers between devices: 37.5 us -> none  [on_device(): lax.all_gather(w_qkv.reshape(w_qkv.shape[0], 3 * group_width), 'dp', axis...]
    all_gather x1, waiting for transfers between devices: 29.8 us -> 0.02 us  [on_device(): out_local = lax.all_gather(w_out, 'dp', axis=1, tiled=True)]
    all_gather x1, waiting for transfers between devices: 33.2 us -> 8.41 us  [on_device(): proj_local = lax.all_gather(w_proj, 'dp', axis=1, tiled=True)]
    ppermute x0 -> x7, starting transfers between devices: none -> 16.4 us  [the longest x3 9.18 us: gather_around(): later.append(lax.ppermute(later[-1], axis, down))]
    ppermute x6, waiting for transfers between devices: 26.9 us -> 12.3 us  [seq_gather(): lax.ppermute(block, 'seq', [(i, (i - shift) % count) for i in range(count)])]
    all_gather x1, waiting for transfers between devices: 4.18 us -> 0.01 us  [on_device(): lax.all_gather(w_glu.reshape(w_glu.shape[0], 2 * group_width), 'dp', axis...]
    unnamed x61 -> x122, local copies, waits for them, and re-layouts: 11.2 us -> 14 us
  transfers between devices with their start and end apart: 16 -> 22, of which waited for: 13 -> 15; matrix products, arithmetic and copies ran while one was open for 17% -> 20% of each run, Pallas kernels for 0% -> 0%
where the time goes in v1:
time: 213 us
  waiting for transfers between devices  116 us (54%)
  starting transfers between devices  30.1 us (14%)
  matrix products  22.5 us (11%)
  local copies, waits for them, and re-layouts  18.5 us (9%)
  between operations  14.1 us (7%)
  other arithmetic  12.2 us (6%)
    ppermute x4, waiting for transfers between devices, gather_around(): earlier.append(lax.ppermute(earlier[-1], axis, up))  56 us
    ppermute x6, waiting for transfers between devices, seq_scatter_sum(): lax.ppermute(piece, 'seq', [(i, (i + shift) % count) for i in range(count)])  33.6 us
    unnamed x122, local copies, waits for them, and re-layouts  14 us
    ppermute x6, waiting for transfers between devices, seq_gather(): lax.ppermute(block, 'seq', [(i, (i - shift) % count) for i in range(count)])  12.3 us
    ppermute x3, starting transfers between devices, gather_around(): later.append(lax.ppermute(later[-1], axis, down))  9.18 us
    all_gather x1, waiting for transfers between devices, on_device(): proj_local = lax.all_gather(w_proj, 'dp', axis=1, tiled=True)  8.41 us
    dot_general x1, matrix products, on_device(): jnp.dot(activated, proj_local, preferred_element_type=jnp.float32)  8.09 us
    ppermute x4, starting transfers between devices, gather_around(): earlier.append(lax.ppermute(earlier[-1], axis, up))  7.25 us
  transfers between devices with their start and end apart: 22, of which 15 were waited for; matrix products, arithmetic and copies ran while one was open for 20% of the time, Pallas kernels for 0%

profile of v1, /device:TPU:1, one launch (start us, length us, event | category | flops | bytes accessed | tf_op | source)
XLA Modules:
  0.0 213.0 jit_solution(2664017020576525598)
XLA Ops:
  13.6 2.7 %collective-permute-start.3 = (bf16[192,1152]{1,0:T(8,128)(2,1)S(1)}, bf16[192,1152]{1,0:T(8,128)(2,1)S(1)}, u32[]{:S(2)}, u32[]{:S(2)}) collective-permute-start(bf16[192,1152]{1,0:T(8,128)(2,1)S(1)} %bitcast.63), channel_id=1, source_target_pairs={{0,4},{4,8},{8,12},{12,16},{16,20},{20,24},{24,28},{28,0},{1,5},{5... | collective-permute-start | bytes 1327112 | tf_op jit(solution)/shard_map/ppermute | solution.py:15
  16.3 3.1 %collective-permute-start.7 = (bf16[192,1152]{1,0:T(8,128)(2,1)S(1)}, bf16[192,1152]{1,0:T(8,128)(2,1)S(1)}, u32[]{:S(2)}, u32[]{:S(2)}) collective-permute-start(bf16[192,1152]{1,0:T(8,128)(2,1)S(1)} %bitcast.64), channel_id=1, source_target_pairs={{0,28},{4,0},{8,4},{12,8},{16,12},{20,16},{24,20},{28,24},{1,29},{... | collective-permute-start | bytes 1327112 | tf_op jit(solution)/shard_map/ppermute | solution.py:17
  24.3 11.6 %collective-permute-done.3 = bf16[192,1152]{1,0:T(8,128)(2,1)S(1)} collective-permute-done((bf16[192,1152]{1,0:T(8,128)(2,1)S(1)}, bf16[192,1152]{1,0:T(8,128)(2,1)S(1)}, u32[]{:S(2)}, u32[]{:S(2)}) %collective-permute-start.3) | collective-permute-done | bytes 442400 | tf_op jit(solution)/shard_map/ppermute | solution.py:15
  39.7 10.2 %collective-permute-done.4 = bf16[192,1152]{1,0:T(8,128)(2,1)S(1)} collective-permute-done((bf16[192,1152]{1,0:T(8,128)(2,1)S(1)}, bf16[192,1152]{1,0:T(8,128)(2,1)S(1)}, u32[]{:S(2)}, u32[]{:S(2)}) %collective-permute-start.4) | collective-permute-done | bytes 442400 | tf_op jit(solution)/shard_map/ppermute | solution.py:15
  51.5 4.2 %collective-permute-start.8 = (bf16[192,1152]{1,0:T(8,128)(2,1)S(1)}, bf16[192,1152]{1,0:T(8,128)(2,1)S(1)}, u32[]{:S(2)}, u32[]{:S(2)}) collective-permute-start(bf16[192,1152]{1,0:T(8,128)(2,1)S(1)} %collective-permute-done.7), channel_id=1, source_target_pairs={{0,28},{4,0},{8,4},{12,8},{16,12},{20,16},{24,20},{28,24},{1,29},{... | collective-permute-start | bytes 1327112 | tf_op jit(solution)/shard_map/ppermute | solution.py:17
  55.7 16.9 %collective-permute-done.5 = bf16[192,1152]{1,0:T(8,128)(2,1)S(1)} collective-permute-done((bf16[192,1152]{1,0:T(8,128)(2,1)S(1)}, bf16[192,1152]{1,0:T(8,128)(2,1)S(1)}, u32[]{:S(2)}, u32[]{:S(2)}) %collective-permute-start.5) | collective-permute-done | bytes 442400 | tf_op jit(solution)/shard_map/ppermute | solution.py:15
  72.5 2.3 %collective-permute-start.6 = (bf16[192,1152]{1,0:T(8,128)(2,1)S(1)}, bf16[192,1152]{1,0:T(8,128)(2,1)S(1)}, u32[]{:S(2)}, u32[]{:S(2)}) collective-permute-start(bf16[192,1152]{1,0:T(8,128)(2,1)S(1)} %collective-permute-done.5), channel_id=1, source_target_pairs={{0,4},{4,8},{8,12},{12,16},{16,20},{20,24},{24,28},{28,0},{1,5},{5... | collective-permute-start | bytes 1327112 | tf_op jit(solution)/shard_map/ppermute | solution.py:15
  78.6 17.2 %collective-permute-done.6 = bf16[192,1152]{1,0:T(8,128)(2,1)S(1)} collective-permute-done((bf16[192,1152]{1,0:T(8,128)(2,1)S(1)}, bf16[192,1152]{1,0:T(8,128)(2,1)S(1)}, u32[]{:S(2)}, u32[]{:S(2)}) %collective-permute-start.6) | collective-permute-done | bytes 442400 | tf_op jit(solution)/shard_map/ppermute | solution.py:15
  96.1 4.2 %collective-permute-done.9 = bf16[192,1152]{1,0:T(8,128)(2,1)S(1)} collective-permute-done((bf16[192,1152]{1,0:T(8,128)(2,1)S(1)}, bf16[192,1152]{1,0:T(8,128)(2,1)S(1)}, u32[]{:S(2)}, u32[]{:S(2)}) %collective-permute-start.9) | collective-permute-done | bytes 442400 | tf_op jit(solution)/shard_map/ppermute | solution.py:17
  102.4 2.2 %fusion.4 = bf16[512,1152]{1,0:T(8,128)(2,1)S(1)} fusion(bf16[3072,1152]{1,0:T(8,128)(2,1)S(1)} %constant_dynamic-update-slice_fusion.8, s32[]{:T(128)S(6)} %select_n.161, bf16[1024,1536]{1,0:T(8,128)(2,1)S(1)} %copy-done.3, s32[]{:T(128)S(6)} %select_n.159), kind=kOutput, calls=%fused_computation.7 | convolution fusion | flops 1812529152 | bytes 6291464 | tf_op jit(solution)/shard_map/dot_general | solution.py:118
  105.2 3.6 %fusion.50 = (f32[4,512]{1,0:T(4,128)S(1)}, f32[4,512,512]{1,2,0:T(8,128)}) fusion(pred[512,512]{0,1:T(8,128)(4,1)S(1)} %broadcast_compare_fusion, bf16[512,3,4,96]{0,3,2,1:T(8,128)(2,1)S(1)} %bitcast.67), kind=kOutput, calls=%fused_computation.173 | convolution fusion | flops 205521408 | bytes 5251072 | tf_op jit(solution)/shard_map/while/body/eval_jaxpr/sub | solution.py:76
  108.9 2.7 %fusion.14 = bf16[4,96,512]{2,1,0:T(8,128)(2,1)S(1)} fusion(f32[4,512,512]{1,2,0:T(8,128)} %get-tuple-element.103, f32[4,512]{1,0:T(4,128)S(1)} %get-tuple-element.102, bf16[512,3,4,96]{0,3,2,1:T(8,128)(2,1)S(1)} %bitcast.68), kind=kOutput, calls=%fused_computation.17 | convolution fusion | flops 203620352 | bytes 4988928 | tf_op jit(solution)/shard_map/while/body/eval_jaxpr/hqk,khe->qhe/dot_general | solution.py:78
  111.6 2.3 %convolution_convert_fusion.1 = bf16[512,1536]{1,0:T(8,128)(2,1)S(1)} fusion(bf16[512,384]{0,1:T(8,128)(2,1)S(1)} %bitcast.71, bf16[384,1536]{0,1:T(8,128)(2,1)} %all-gather.4.cloned.1.call-done), kind=kOutput, calls=%fused_computation.9 | convolution fusion | flops 604766208 | bytes 3145728 | tf_op jit(solution)/shard_map/dot_general | solution.py:124
  114.1 3.0 %collective-permute-start.10 = (bf16[128,1536]{1,0:T(8,128)(2,1)S(1)}, bf16[128,1536]{1,0:T(8,128)(2,1)S(1)}, u32[]{:S(2)}, u32[]{:S(2)}) collective-permute-start(bf16[128,1536]{1,0:T(8,128)(2,1)S(1)} %get-tuple-element.68), channel_id=1, source_target_pairs={{0,1},{1,2},{2,3},{3,0},{4,5},{5,6},{6,7},{7,4},{8,9},{9,10},{10,1... | collective-permute-start | bytes 1179656 | tf_op jit(solution)/shard_map/ppermute | solution.py:51
  119.1 6.3 %collective-permute-done.10 = bf16[128,1536]{1,0:T(8,128)(2,1)S(1)} collective-permute-done((bf16[128,1536]{1,0:T(8,128)(2,1)S(1)}, bf16[128,1536]{1,0:T(8,128)(2,1)S(1)}, u32[]{:S(2)}, u32[]{:S(2)}) %collective-permute-start.10) | collective-permute-done | bytes 393248 | tf_op jit(solution)/shard_map/ppermute | solution.py:51
  125.4 9.0 %collective-permute-done.11 = bf16[128,1536]{1,0:T(8,128)(2,1)} collective-permute-done((bf16[128,1536]{1,0:T(8,128)(2,1)S(1)}, bf16[128,1536]{1,0:T(8,128)(2,1)}, u32[]{:S(2)}, u32[]{:S(2)}) %collective-permute-start.11) | collective-permute-done | bytes 393248 | tf_op jit(solution)/shard_map/ppermute | solution.py:51
  143.3 5.6 %collective-permute-done.13 = bf16[128,1536]{1,0:T(8,128)(2,1)S(1)} collective-permute-done((bf16[128,1536]{1,0:T(8,128)(2,1)S(1)}, bf16[128,1536]{1,0:T(8,128)(2,1)S(1)}, u32[]{:S(2)}, u32[]{:S(2)}) %collective-permute-start.13) | collective-permute-done | bytes 393248 | tf_op jit(solution)/shard_map/ppermute | solution.py:38
  150.5 6.6 %collective-permute-done.15 = bf16[128,1536]{1,0:T(8,128)(2,1)S(1)} collective-permute-done((bf16[128,1536]{1,0:T(8,128)(2,1)S(1)}, bf16[128,1536]{1,0:T(8,128)(2,1)S(1)}, u32[]{:S(2)}, u32[]{:S(2)}) %collective-permute-start.15) | collective-permute-done | bytes 393248 | tf_op jit(solution)/shard_map/ppermute | solution.py:38
  161.1 3.5 %fusion.11 = f32[512,768]{1,0:T(8,128)S(1)} fusion(bf16[1536,768]{1,0:T(8,128)(2,1)} %all-gather.6.cloned.1.call-done, bf16[1024,1536]{1,0:T(8,128)(2,1)} %constant_dynamic-update-slice_fusion.24, s32[]{:T(128)S(6)} %select_n.159), kind=kOutput, calls=%fused_computation.14 | convolution fusion | flops 1207959552 | bytes 5505028 | tf_op jit(solution)/shard_map/dot_general | solution.py:129
  167.3 8.4 %all-gather.8.cloned.1.call-done = bf16[384,1536]{0,1:T(8,128)(2,1)} async-done(((bf16[384,192]{0,1:T(8,128)(2,1)}), bf16[384,1536]{0,1:T(8,128)(2,1)}) %all-gather.8.cloned.1.call-update) | async-done | bytes 1179664 | tf_op jit(solution)/shard_map/all_gather | solution.py:112
  176.1 8.1 %convolution_convert_fusion = bf16[512,1536]{1,0:T(8,128)(2,1)S(1)} fusion(bf16[384,1536]{0,1:T(8,128)(2,1)} %all-gather.8.cloned.1.call-done, bf16[512,384]{1,0:T(8,128)(2,1)S(1)} %fusion.37, f32[384]{0:T(512)S(1)} %copy-done.31, f32[384]{0:T(512)S(1)} %copy-done.32, f32[384]{0:T(512)S(1)} %get-tuple-element.18, f32[384]{0:T(512)S(1)} %get-tuple-element.19, ...), kind=kOutput, calls=%fused_computation.8 | convolution fusion | flops 629932032 | bytes 3209216 | tf_op jit(solution)/shard_map/dot_general | solution.py:139
  184.3 3.0 %collective-permute-start.16 = (bf16[128,1536]{1,0:T(8,128)(2,1)S(1)}, bf16[128,1536]{1,0:T(8,128)(2,1)S(1)}, u32[]{:S(2)}, u32[]{:S(2)}) collective-permute-start(bf16[128,1536]{1,0:T(8,128)(2,1)S(1)} %get-tuple-element.63), channel_id=1, source_target_pairs={{0,1},{1,2},{2,3},{3,0},{4,5},{5,6},{6,7},{7,4},{8,9},{9,10},{10,1... | collective-permute-start | bytes 1179656 | tf_op jit(solution)/shard_map/ppermute | solution.py:51
  187.8 7.9 %collective-permute-done.16 = bf16[128,1536]{1,0:T(8,128)(2,1)S(1)} collective-permute-done((bf16[128,1536]{1,0:T(8,128)(2,1)S(1)}, bf16[128,1536]{1,0:T(8,128)(2,1)S(1)}, u32[]{:S(2)}, u32[]{:S(2)}) %collective-permute-start.16) | collective-permute-done | bytes 393248 | tf_op jit(solution)/shard_map/ppermute | solution.py:51
  195.7 9.1 %collective-permute-done.17 = bf16[128,1536]{1,0:T(8,128)(2,1)S(1)} collective-permute-done((bf16[128,1536]{1,0:T(8,128)(2,1)S(1)}, bf16[128,1536]{1,0:T(8,128)(2,1)S(1)}, u32[]{:S(2)}, u32[]{:S(2)}) %collective-permute-start.17) | collective-permute-done | bytes 393248 | tf_op jit(solution)/shard_map/ppermute | solution.py:51
  (181 shorter events, 44.8 us)
Async XLA Ops:
  6.5 105.0 %all-gather.4.cloned.1.call-start = ((), (), s32[]{:S(2)}) async-start(), calls=%async_computation | async-start | bytes 1327104 | tf_op jit(solution)/shard_map/all_gather | solution.py:108
  7.3 153.8 %all-gather.6.cloned.1.call-start = ((), (), s32[]{:S(2)}) async-start(), calls=%async_computation.1 | async-start | bytes 2654208 | tf_op jit(solution)/shard_map/all_gather | solution.py:109
  9.0 166.7 %all-gather.8.cloned.1.call-start = ((), (), s32[]{:S(2)}) async-start(), calls=%async_computation.2 | async-start | bytes 1327104 | tf_op jit(solution)/shard_map/all_gather | solution.py:112
  13.4 10.0 %collective-permute-start = (bf16[128,1536]{1,0:T(8,128)(2,1)S(1)}, bf16[128,1536]{1,0:T(8,128)(2,1)S(1)}, u32[]{:S(2)}, u32[]{:S(2)}) collective-permute-start(bf16[128,1536]{1,0:T(8,128)(2,1)S(1)} %get-tuple-element.62), channel_id=1, source_target_pairs={{0,3},{1,0},{2,1},{3,2},{4,7},{5,4},{6,5},{7,6},{8,11},{9,8},{10,9... | collective-permute-start | bytes 1179656 | tf_op jit(solution)/shard_map/ppermute | solution.py:38
  13.6 22.3 %collective-permute-start.3 = (bf16[192,1152]{1,0:T(8,128)(2,1)S(1)}, bf16[192,1152]{1,0:T(8,128)(2,1)S(1)}, u32[]{:S(2)}, u32[]{:S(2)}) collective-permute-start(bf16[192,1152]{1,0:T(8,128)(2,1)S(1)} %bitcast.63), channel_id=1, source_target_pairs={{0,4},{4,8},{8,12},{12,16},{16,20},{20,24},{24,28},{28,0},{1,5},{5... | collective-permute-start | bytes 1327112 | tf_op jit(solution)/shard_map/ppermute | solution.py:15
  16.3 35.2 %collective-permute-start.7 = (bf16[192,1152]{1,0:T(8,128)(2,1)S(1)}, bf16[192,1152]{1,0:T(8,128)(2,1)S(1)}, u32[]{:S(2)}, u32[]{:S(2)}) collective-permute-start(bf16[192,1152]{1,0:T(8,128)(2,1)S(1)} %bitcast.64), channel_id=1, source_target_pairs={{0,28},{4,0},{8,4},{12,8},{16,12},{20,16},{24,20},{28,24},{1,29},{... | collective-permute-start | bytes 1327112 | tf_op jit(solution)/shard_map/ppermute | solution.py:17
  19.4 18.7 %collective-permute-start.1 = (bf16[128,1536]{1,0:T(8,128)(2,1)S(1)}, bf16[128,1536]{1,0:T(8,128)(2,1)S(1)}, u32[]{:S(2)}, u32[]{:S(2)}) collective-permute-start(bf16[128,1536]{1,0:T(8,128)(2,1)S(1)} %get-tuple-element.62), channel_id=1, source_target_pairs={{0,2},{1,3},{2,0},{3,1},{4,6},{5,7},{6,4},{7,5},{8,10},{9,11},{10,... | collective-permute-start | bytes 1179656 | tf_op jit(solution)/shard_map/ppermute | solution.py:38
  20.6 18.2 %collective-permute-start.2 = (bf16[128,1536]{1,0:T(8,128)(2,1)S(1)}, bf16[128,1536]{1,0:T(8,128)(2,1)S(1)}, u32[]{:S(2)}, u32[]{:S(2)}) collective-permute-start(bf16[128,1536]{1,0:T(8,128)(2,1)S(1)} %get-tuple-element.62), channel_id=1, source_target_pairs={{0,1},{1,2},{2,3},{3,0},{4,5},{5,6},{6,7},{7,4},{8,9},{9,10},{10,1... | collective-permute-start | bytes 1179656 | tf_op jit(solution)/shard_map/ppermute | solution.py:38
  35.9 14.0 %collective-permute-start.4 = (bf16[192,1152]{1,0:T(8,128)(2,1)S(1)}, bf16[192,1152]{1,0:T(8,128)(2,1)S(1)}, u32[]{:S(2)}, u32[]{:S(2)}) collective-permute-start(bf16[192,1152]{1,0:T(8,128)(2,1)S(1)} %collective-permute-done.3), channel_id=1, source_target_pairs={{0,4},{4,8},{8,12},{12,16},{16,20},{20,24},{24,28},{28,0},{1,5},{5... | collective-permute-start | bytes 1327112 | tf_op jit(solution)/shard_map/ppermute | solution.py:15
  49.9 22.6 %collective-permute-start.5 = (bf16[192,1152]{1,0:T(8,128)(2,1)S(1)}, bf16[192,1152]{1,0:T(8,128)(2,1)S(1)}, u32[]{:S(2)}, u32[]{:S(2)}) collective-permute-start(bf16[192,1152]{1,0:T(8,128)(2,1)S(1)} %collective-permute-done.4), channel_id=1, source_target_pairs={{0,4},{4,8},{8,12},{12,16},{16,20},{20,24},{24,28},{28,0},{1,5},{5... | collective-permute-start | bytes 1327112 | tf_op jit(solution)/shard_map/ppermute | solution.py:15
  51.5 25.2 %collective-permute-start.8 = (bf16[192,1152]{1,0:T(8,128)(2,1)S(1)}, bf16[192,1152]{1,0:T(8,128)(2,1)S(1)}, u32[]{:S(2)}, u32[]{:S(2)}) collective-permute-start(bf16[192,1152]{1,0:T(8,128)(2,1)S(1)} %collective-permute-done.7), channel_id=1, source_target_pairs={{0,28},{4,0},{8,4},{12,8},{16,12},{20,16},{24,20},{28,24},{1,29},{... | collective-permute-start | bytes 1327112 | tf_op jit(solution)/shard_map/ppermute | solution.py:17
  72.5 23.3 %collective-permute-start.6 = (bf16[192,1152]{1,0:T(8,128)(2,1)S(1)}, bf16[192,1152]{1,0:T(8,128)(2,1)S(1)}, u32[]{:S(2)}, u32[]{:S(2)}) collective-permute-start(bf16[192,1152]{1,0:T(8,128)(2,1)S(1)} %collective-permute-done.5), channel_id=1, source_target_pairs={{0,4},{4,8},{8,12},{12,16},{16,20},{20,24},{24,28},{28,0},{1,5},{5... | collective-permute-start | bytes 1327112 | tf_op jit(solution)/shard_map/ppermute | solution.py:15
  76.6 23.7 %collective-permute-start.9 = (bf16[192,1152]{1,0:T(8,128)(2,1)S(1)}, bf16[192,1152]{1,0:T(8,128)(2,1)S(1)}, u32[]{:S(2)}, u32[]{:S(2)}) collective-permute-start(bf16[192,1152]{1,0:T(8,128)(2,1)S(1)} %collective-permute-done.8), channel_id=1, source_target_pairs={{0,28},{4,0},{8,4},{12,8},{16,12},{20,16},{24,20},{28,24},{1,29},{... | collective-permute-start | bytes 1327112 | tf_op jit(solution)/shard_map/ppermute | solution.py:17
  111.5 23.5 %copy-start = (bf16[1,128,1536]{2,1,0:T(8,128)(2,1)S(1)}, bf16[1,128,1536]{2,1,0:T(8,128)(2,1)}, u32[]{:S(2)}) copy-start(bf16[1,128,1536]{2,1,0:T(8,128)(2,1)} %param.9) | copy-start | bytes 1179652
  113.9 22.9 %copy-start.4 = (f32[1536]{0:T(1024)S(1)}, f32[1536]{0:T(1024)}, u32[]{:S(2)}) copy-start(f32[1536]{0:T(1024)} %param.12) | copy-start | bytes 18436
  114.1 11.3 %collective-permute-start.10 = (bf16[128,1536]{1,0:T(8,128)(2,1)S(1)}, bf16[128,1536]{1,0:T(8,128)(2,1)S(1)}, u32[]{:S(2)}, u32[]{:S(2)}) collective-permute-start(bf16[128,1536]{1,0:T(8,128)(2,1)S(1)} %get-tuple-element.68), channel_id=1, source_target_pairs={{0,1},{1,2},{2,3},{3,0},{4,5},{5,6},{6,7},{7,4},{8,9},{9,10},{10,1... | collective-permute-start | bytes 1179656 | tf_op jit(solution)/shard_map/ppermute | solution.py:51
  117.1 17.3 %collective-permute-start.11 = (bf16[128,1536]{1,0:T(8,128)(2,1)S(1)}, bf16[128,1536]{1,0:T(8,128)(2,1)}, u32[]{:S(2)}, u32[]{:S(2)}) collective-permute-start(bf16[128,1536]{1,0:T(8,128)(2,1)S(1)} %get-tuple-element.70), channel_id=1, source_target_pairs={{0,2},{1,3},{2,0},{3,1},{4,6},{5,7},{6,4},{7,5},{8,10},{9,11},{10,... | collective-permute-start | bytes 1179656 | tf_op jit(solution)/shard_map/ppermute | solution.py:51
  117.1 17.9 %collective-permute-start.12 = (bf16[128,1536]{1,0:T(8,128)(2,1)S(1)}, bf16[128,1536]{1,0:T(8,128)(2,1)}, u32[]{:S(2)}, u32[]{:S(2)}) collective-permute-start(bf16[128,1536]{1,0:T(8,128)(2,1)S(1)} %get-tuple-element.69), channel_id=1, source_target_pairs={{0,3},{1,0},{2,1},{3,2},{4,7},{5,4},{6,5},{7,6},{8,11},{9,8},{10,9... | collective-permute-start | bytes 1179656 | tf_op jit(solution)/shard_map/ppermute | solution.py:51
  137.7 11.2 %collective-permute-start.13 = (bf16[128,1536]{1,0:T(8,128)(2,1)S(1)}, bf16[128,1536]{1,0:T(8,128)(2,1)S(1)}, u32[]{:S(2)}, u32[]{:S(2)}) collective-permute-start(bf16[128,1536]{1,0:T(8,128)(2,1)S(1)} %get-tuple-element.58), channel_id=1, source_target_pairs={{0,3},{1,0},{2,1},{3,2},{4,7},{5,4},{6,5},{7,6},{8,11},{9,8},{10,9... | collective-permute-start | bytes 1179656 | tf_op jit(solution)/shard_map/ppermute | solution.py:38
  138.4 11.3 %collective-permute-start.14 = (bf16[128,1536]{1,0:T(8,128)(2,1)S(1)}, bf16[128,1536]{1,0:T(8,128)(2,1)S(1)}, u32[]{:S(2)}, u32[]{:S(2)}) collective-permute-start(bf16[128,1536]{1,0:T(8,128)(2,1)S(1)} %get-tuple-element.58), channel_id=1, source_target_pairs={{0,2},{1,3},{2,0},{3,1},{4,6},{5,7},{6,4},{7,5},{8,10},{9,11},{10,... | collective-permute-start | bytes 1179656 | tf_op jit(solution)/shard_map/ppermute | solution.py:38
  141.3 15.9 %collective-permute-start.15 = (bf16[128,1536]{1,0:T(8,128)(2,1)S(1)}, bf16[128,1536]{1,0:T(8,128)(2,1)S(1)}, u32[]{:S(2)}, u32[]{:S(2)}) collective-permute-start(bf16[128,1536]{1,0:T(8,128)(2,1)S(1)} %get-tuple-element.58), channel_id=1, source_target_pairs={{0,1},{1,2},{2,3},{3,0},{4,5},{5,6},{6,7},{7,4},{8,9},{9,10},{10,1... | collective-permute-start | bytes 1179656 | tf_op jit(solution)/shard_map/ppermute | solution.py:38
  184.3 11.4 %collective-permute-start.16 = (bf16[128,1536]{1,0:T(8,128)(2,1)S(1)}, bf16[128,1536]{1,0:T(8,128)(2,1)S(1)}, u32[]{:S(2)}, u32[]{:S(2)}) collective-permute-start(bf16[128,1536]{1,0:T(8,128)(2,1)S(1)} %get-tuple-element.63), channel_id=1, source_target_pairs={{0,1},{1,2},{2,3},{3,0},{4,5},{5,6},{6,7},{7,4},{8,9},{9,10},{10,1... | collective-permute-start | bytes 1179656 | tf_op jit(solution)/shard_map/ppermute | solution.py:51
  187.4 17.5 %collective-permute-start.17 = (bf16[128,1536]{1,0:T(8,128)(2,1)S(1)}, bf16[128,1536]{1,0:T(8,128)(2,1)S(1)}, u32[]{:S(2)}, u32[]{:S(2)}) collective-permute-start(bf16[128,1536]{1,0:T(8,128)(2,1)S(1)} %get-tuple-element.65), channel_id=1, source_target_pairs={{0,2},{1,3},{2,0},{3,1},{4,6},{5,7},{6,4},{7,5},{8,10},{9,11},{10,... | collective-permute-start | bytes 1179656 | tf_op jit(solution)/shard_map/ppermute | solution.py:51
  187.6 17.8 %collective-permute-start.18 = (bf16[128,1536]{1,0:T(8,128)(2,1)S(1)}, bf16[128,1536]{1,0:T(8,128)(2,1)S(1)}, u32[]{:S(2)}, u32[]{:S(2)}) collective-permute-start(bf16[128,1536]{1,0:T(8,128)(2,1)S(1)} %get-tuple-element.64), channel_id=1, source_target_pairs={{0,3},{1,0},{2,1},{3,2},{4,7},{5,4},{6,5},{7,6},{8,11},{9,8},{10,9... | collective-permute-start | bytes 1179656 | tf_op jit(solution)/shard_map/ppermute | solution.py:51
  (45 other events, 457.0 us)
Sparse Core Ops, SparseCore 0:
  9.5 65.5 all-gather.3
  77.3 56.6 all-gather.5
  136.2 39.4 all-gather.7
